TPU v7x, 512 devices: a whole 4x4x16 slice. The times are simulated.
512 devices in a mesh: win: 16 (over z_hi, y, core), tm: 32 (over z_lo, x).
Axes of the slice: x: 4, y: 4, z: 16 (z_hi: 2, z_lo: 8; z = z_hi * 8 + z_lo), core: 2. Of those that a mesh axis runs over, the one named last changes fastest.
Arguments:
- frame_inputs: bfloat16 [16, 4096, 2048], P('win', 'tm'), may hold values from -6 to 6
- gate_channels: bfloat16 [16, 4096, 2048], P('win', 'tm'), may hold values from -6 to 6
- state_input_weight: bfloat16 [16, 4096, 128], P('win', 'tm'), may hold values from -6 to 6
- state_output_weight: bfloat16 [16, 4096, 128], P('win', 'tm'), may hold values from -0.59765625 to 0.59765625
- head_decay_codes: int32 [2, 32], replicated, may hold values from 0 to 7
- loss_frames: int32 [16, 4096], P('win', 'tm'), may hold values 0 or 1
- gated_norm_gain: float32 [2048], replicated, may hold values from 0.1 to 1.9
- output_weight: bfloat16 [2048, 1024], P(None, 'tm'), may hold values from -0.125 to 0.125
- seam_taper_shape: int32 [16], replicated, may hold values from 0 to 3
Outputs:
- mixed: bfloat16 [16, 4096, 1024], P('win', 'tm')
All inputs are finite; a program needn't handle non-finite values. No bound on the sum of `loss_frames` on one device may be relied on, other than what follows from the above.
Results may differ from a plain program's by a relative error of at most 0.0059.
Values may be sent and summed in bfloat16 or wider, within the bound.
No kernel may reach another device: no remote copies, remote signals or barrier semaphores. Data moves between devices by JAX's collectives and lax.ppermute only.
A program may use at most 192 MiB of HBM per device.

v0:
```python
import jax
import jax.numpy as jnp
from jax import lax
from jax.sharding import PartitionSpec as P

H = 32
P_SIZE = 64
N = 128
SEAM_DEVS = 4
STATE_LOSS = 0.4
EPSILON = 1e-05


def prefix(value, axis, join, neutral, backward):
    count, mine = (lax.axis_size(axis), lax.axis_index(axis))
    pieces = jax.tree.map(lambda part: lax.all_gather(part, axis), value)
    if backward:
        pieces = jax.tree.map(lambda part: part[::-1], pieces)
        mine = count - 1 - mine
    total = jax.tree.map(
        lambda part, zero: jnp.full_like(part, 0) + jnp.asarray(zero, part.dtype), value, neutral
    )

    def lap(position, total):
        longer = join(total, jax.tree.map(lambda part: part[position], pieces))
        return jax.tree.map(lambda new, old: jnp.where(position < mine, new, old), longer, total)

    return lax.fori_loop(0, count - 1, lap, total)


def shifted(array, axis, by):
    count = lax.axis_size(axis)
    pairs = [(i, i + by) for i in range(count) if 0 <= i + by < count]
    return lax.ppermute(array, axis, pairs)


def decay_rates(head_decay_codes, window_length):
    codes_float = head_decay_codes.astype(jnp.float32)
    quick = jnp.exp2(-codes_float) / 32.0
    gentle = jnp.exp2(5.0 - codes_float) / window_length
    return jnp.where(head_decay_codes < 4, quick, gentle)


def taper_weight(taper_code, position, seam_length):
    spread = (position.astype(jnp.float32) + 0.5) / seam_length
    shapes = jnp.stack(
        [
            spread,
            spread * spread * (3.0 - 2.0 * spread),
            jnp.sin(0.5 * jnp.pi * spread) ** 2,
            spread**3 * (spread * (6.0 * spread - 15.0) + 10.0),
        ]
    )
    kind_index = jnp.arange(4).reshape((4,) + (1,) * spread.ndim)
    selected = kind_index == jnp.expand_dims(taper_code, 0)
    return jnp.sum(jnp.where(selected, shapes, 0.0), axis=0)


def link_states(earlier, later):
    return (earlier[0] * later[0], later[0][:, None, None] * earlier[1] + later[1])


def per_device(
    frame_inputs,
    gate_channels,
    state_input_weight,
    state_output_weight,
    head_decay_codes,
    loss_frames,
    gated_norm_gain,
    output_weight,
    seam_taper_shape,
):
    frames = frame_inputs[0]
    frame_count = frames.shape[0]
    chain_length = lax.axis_size("tm")
    window_length = frame_count * chain_length
    seam_length = SEAM_DEVS * frame_count
    stride_length = window_length - seam_length
    reach = chain_length - SEAM_DEVS
    group_count = H // 4
    decay_rate_pair = decay_rates(head_decay_codes, window_length)
    loss_float = loss_frames[0].astype(jnp.float32)[:, None]
    forward_log_decay = -(decay_rate_pair[0][None, :] + STATE_LOSS * loss_float)
    backward_log_decay = -(decay_rate_pair[1][None, :] + STATE_LOSS * loss_float)
    running_fwd = jnp.cumsum(forward_log_decay, axis=0)
    running_bwd = jnp.flip(jnp.cumsum(jnp.flip(backward_log_decay, 0), axis=0), 0)
    b_rows = state_input_weight[0]
    c_rows = state_output_weight[0]
    head_frames = frames.reshape(frame_count, H, P_SIZE)
    b_float = b_rows.astype(jnp.float32)[:, None, :]
    weighted_fwd = (jnp.exp(running_fwd[-1][None, :] - running_fwd)[:, :, None] * b_float).astype(
        jnp.bfloat16
    )
    weighted_bwd = (jnp.exp(running_bwd[0][None, :] - running_bwd)[:, :, None] * b_float).astype(
        jnp.bfloat16
    )
    fresh_fwd = jnp.einsum(
        "shp,shn->hpn", head_frames, weighted_fwd, preferred_element_type=jnp.float32
    )
    fresh_bwd = jnp.einsum(
        "shp,shn->hpn", head_frames, weighted_bwd, preferred_element_type=jnp.float32
    )
    identity_pair = (jnp.ones((H,), jnp.float32), jnp.zeros((H, P_SIZE, N), jnp.float32))
    _, state_fwd = prefix(
        (jnp.exp(running_fwd[-1]), fresh_fwd), "tm", link_states, identity_pair, False
    )
    _, state_bwd = prefix(
        (jnp.exp(running_bwd[0]), fresh_bwd), "tm", link_states, identity_pair, True
    )
    scores = jnp.dot(c_rows, b_rows.T, preferred_element_type=jnp.float32)
    lower_mask = jnp.arange(frame_count)[:, None] >= jnp.arange(frame_count)[None, :]

    def group_mix(group_items):
        group_fwd, group_bwd, group_frames = group_items
        exponent = jnp.where(
            lower_mask[None],
            group_fwd[:, :, None] - group_fwd[:, None, :],
            group_bwd[:, :, None] - group_bwd[:, None, :],
        )
        mixing = (scores[None] * jnp.exp(exponent)).astype(jnp.bfloat16)
        return jnp.einsum("hts,shp->thp", mixing, group_frames, preferred_element_type=jnp.float32)

    grouped_fwd = running_fwd.T.reshape(group_count, 4, frame_count)
    grouped_bwd = running_bwd.T.reshape(group_count, 4, frame_count)
    grouped_frames = head_frames.reshape(frame_count, group_count, 4, P_SIZE).transpose(1, 0, 2, 3)
    local_groups = lax.map(group_mix, (grouped_fwd, grouped_bwd, grouped_frames))
    local_part = local_groups.transpose(1, 0, 2, 3).reshape(frame_count, H, P_SIZE)
    c_float = c_rows.astype(jnp.float32)
    carried_fwd = jnp.exp(running_fwd)[:, :, None] * jnp.einsum(
        "hpn,tn->thp", state_fwd, c_float, precision=lax.Precision.HIGHEST
    )
    carried_bwd = jnp.exp(running_bwd)[:, :, None] * jnp.einsum(
        "hpn,tn->thp", state_bwd, c_float, precision=lax.Precision.HIGHEST
    )
    summed = local_part + carried_fwd + carried_bwd
    gated_rows = summed * jax.nn.silu(gate_channels[0].astype(jnp.float32)).reshape(
        frame_count, H, P_SIZE
    )
    inverse_rms = lax.rsqrt(jnp.mean(gated_rows * gated_rows, axis=-1, keepdims=True) + EPSILON)
    normed = (
        (gated_rows * inverse_rms).reshape(frame_count, H * P_SIZE) * gated_norm_gain[None, :]
    ).astype(jnp.bfloat16)
    projected_rows = jnp.dot(
        normed,
        lax.all_gather(output_weight, "tm", axis=1, tiled=True),
        preferred_element_type=jnp.float32,
    ).astype(jnp.bfloat16)
    across_previous = shifted(projected_rows, "win", 1)
    from_previous = shifted(across_previous, "tm", -reach)
    across_next = shifted(projected_rows, "win", -1)
    from_next = shifted(across_next, "tm", reach)
    window_index = lax.axis_index("win")
    window_total = lax.axis_size("win")
    position = lax.axis_index("tm") * frame_count + jnp.arange(frame_count)
    next_window = jnp.minimum(window_index + 1, window_total - 1)
    head_fade = taper_weight(seam_taper_shape[window_index], position, seam_length)[:, None]
    tail_fade = taper_weight(seam_taper_shape[next_window], position - stride_length, seam_length)[
        :, None
    ]
    own_rows = projected_rows.astype(jnp.float32)
    head_mix = head_fade * own_rows + (1.0 - head_fade) * from_previous.astype(jnp.float32)
    tail_mix = tail_fade * from_next.astype(jnp.float32) + (1.0 - tail_fade) * own_rows
    use_head = (position < seam_length) & (window_index > 0)
    use_tail = (position >= stride_length) & (window_index < window_total - 1)
    mixed = jnp.where(use_head[:, None], head_mix, jnp.where(use_tail[:, None], tail_mix, own_rows))
    return mixed.astype(jnp.bfloat16)[None]


def solution(mesh):
    in_specs = (
        P("win", "tm", None),
        P("win", "tm", None),
        P("win", "tm", None),
        P("win", "tm", None),
        P(),
        P("win", "tm"),
        P(),
        P(None, "tm"),
        P(),
    )
    out_specs = P("win", "tm", None)
    return jax.shard_map(
        per_device, mesh=mesh, in_specs=in_specs, out_specs=out_specs, check_vma=False
    )
```

profile of v0, /device:TPU:480, one launch (start us, length us, event | category | flops | bytes accessed | tf_op | source)
XLA Modules:
  0.0 1035.5 jit_solution(9995021697445433449)
XLA Ops:
  10.5 1.8 convolution_bitcast_fusion.4
  13.0 1.8 convolution_bitcast_fusion.3
  15.7 98.1 %all-gather.2 = f32[32,1,32]{2,1,0:T(1,128)S(1)} all-gather(f32[1,1,32]{2,1,0:T(1,128)S(1)} %get-tuple-element.328), channel_id=1, replica_groups=mesh['win'=16,'tm'=32] {'tm'}, dimensions={0}, use_global_device_ids=true | all-gather | bytes 4224 | tf_op jit(solution)/shard_map/all_gather | solution.py:16
  114.1 8.2 while.39
  122.3 116.8 %all-gather.3 = f32[32,1,32]{2,1,0:T(1,128)S(1)} all-gather(f32[1,1,32]{2,1,0:T(1,128)S(1)} %get-tuple-element.324), channel_id=1, replica_groups=mesh['win'=16,'tm'=32] {'tm'}, dimensions={0}, use_global_device_ids=true | all-gather | bytes 4224 | tf_op jit(solution)/shard_map/all_gather | solution.py:16
  242.3 139.6 %all-gather.10.cloned.1.call-done = f32[1024,64,128]{2,1,0:T(8,128)} async-done(((f32[32,64,128]{2,1,0:T(8,128)}), f32[1024,64,128]{2,1,0:T(8,128)}) %all-gather.10.cloned.1.call-update) | async-done | bytes 33554448 | tf_op jit(solution)/shard_map/all_gather | solution.py:16
  381.9 46.8 %while.40 = (s32[]{:T(128)}, f32[32,64,128]{2,1,0:T(8,128)S(1)}, s32[]{:T(128)}, f32[32,32]{1,0:T(8,128)S(1)}, f32[32,32,64,128]{3,2,1,0:T(8,128)}, /*index=5*/s32[]{:T(128)}, s32[]{:T(128)}) while((s32[]{:T(128)}, f32[32,64,128]{2,1,0:T(8,128)S(1)}, s32[]{:T(128)}, f32[32,32]{1,0:T(8,128)S(1)}, f32[32,32,64,128]{3,2,1,0:T(8,128)}, ...), condition=%wide.region_6.7_spmd.clone, body=%wide.region_5.6_spmd.clone.sunk | while | flops 1048580 | bytes 3146217 | solution.py:28
  383.4 1.5 fusion.53
  384.9 1.5 fusion.53
  386.4 1.5 fusion.53
  387.9 1.5 fusion.53
  389.4 1.5 fusion.53
  390.9 1.5 fusion.53
  392.5 1.5 fusion.53
  394.0 1.5 fusion.53
  395.5 1.5 fusion.53
  398.5 1.5 fusion.53
  400.0 1.5 fusion.53
  401.5 1.5 fusion.53
  403.0 1.5 fusion.53
  404.5 1.5 fusion.53
  406.0 1.5 fusion.53
  407.5 1.5 fusion.53
  409.1 1.5 fusion.53
  410.6 1.5 fusion.53
  412.1 1.5 fusion.53
  413.6 1.5 fusion.53
  415.1 1.5 fusion.53
  416.6 1.5 fusion.53
  418.1 1.5 fusion.53
  419.6 1.5 fusion.53
  421.2 1.5 fusion.53
  422.7 1.5 fusion.53
  424.2 1.5 fusion.53
  425.7 1.5 fusion.53
  427.2 1.5 fusion.53
  428.7 324.4 %all-gather.12.cloned.1.call-done = f32[1024,64,128]{2,1,0:T(8,128)} async-done(((f32[32,64,128]{2,1,0:T(8,128)}), f32[1024,64,128]{2,1,0:T(8,128)}) %all-gather.12.cloned.1.call-update) | async-done | bytes 33554448 | tf_op jit(solution)/shard_map/all_gather | solution.py:16
  753.1 23.3 %rev.16 = f32[32,32,64,128]{3,2,1,0:T(8,128)} reverse(f32[32,32,64,128]{3,2,1,0:T(8,128)} %bitcast.116), dimensions={0} | reverse | bytes 67108864 | tf_op jit(solution)/shard_map/rev | solution.py:18
  776.4 1.8 fusion.17
  778.2 46.8 %while.41 = (s32[]{:T(128)}, f32[32,64,128]{2,1,0:T(8,128)S(1)}, s32[]{:T(128)}, f32[32,32]{1,0:T(8,128)S(1)}, f32[32,32,64,128]{3,2,1,0:T(8,128)}, /*index=5*/s32[]{:T(128)}, s32[]{:T(128)}) while((s32[]{:T(128)}, f32[32,64,128]{2,1,0:T(8,128)S(1)}, s32[]{:T(128)}, f32[32,32]{1,0:T(8,128)S(1)}, f32[32,32,64,128]{3,2,1,0:T(8,128)}, ...), condition=%wide.region_8.9_spmd.clone, body=%wide.region_7.8_spmd.clone.sunk | while | flops 1048580 | bytes 3146217 | solution.py:28
  778.3 1.6 fusion.54
  779.9 1.5 fusion.54
  781.4 1.5 fusion.54
  782.9 1.5 fusion.54
  784.4 1.5 fusion.54
  785.9 1.5 fusion.54
  787.4 1.5 fusion.54
  788.9 1.5 fusion.54
  790.4 1.5 fusion.54
  791.9 1.5 fusion.54
  794.9 1.5 fusion.54
  797.9 1.5 fusion.54
  805.5 1.5 fusion.54
  810.0 1.5 fusion.54
  813.0 1.5 fusion.54
  820.5 1.5 fusion.54
  826.4 145.4 %all-gather.8.cloned.1.call-done = bf16[2048,1024]{0,1:T(8,128)(2,1)} async-done(((bf16[2048,32]{0,1:T(8,128)(2,1)}), bf16[2048,1024]{0,1:T(8,128)(2,1)}) %all-gather.8.cloned.1.call-update) | async-done | bytes 4194320 | tf_op jit(solution)/shard_map/all_gather | solution.py:146
  971.8 3.7 convolution_convert_fusion
  975.5 1.9 collective-permute-start
  977.4 14.5 %collective-permute-start.2 = (bf16[128,1024]{1,0:T(8,128)(2,1)S(1)}, bf16[128,1024]{1,0:T(8,128)(2,1)S(1)}, u32[]{:S(2)}, u32[]{:S(2)}) collective-permute-start(bf16[128,1024]{1,0:T(8,128)(2,1)S(1)} %convolution_convert_fusion), channel_id=1, source_target_pairs={{32,0},{64,32},{96,64},{128,96},{160,128},{192,160},{224,192},{256... | collective-permute-start | bytes 786440 | tf_op jit(solution)/shard_map/ppermute | solution.py:34
  992.0 2.0 collective-permute-done
  994.0 19.1 %collective-permute-start.1 = (bf16[128,1024]{1,0:T(8,128)(2,1)S(1)}, bf16[128,1024]{1,0:T(8,128)(2,1)S(1)}, u32[]{:S(2)}, u32[]{:S(2)}) collective-permute-start(bf16[128,1024]{1,0:T(8,128)(2,1)S(1)} %collective-permute-done), channel_id=1, source_target_pairs={{28,0},{29,1},{30,2},{31,3},{60,32},{61,33},{62,34},{63,35},{92,64... | collective-permute-start | bytes 786440 | tf_op jit(solution)/shard_map/ppermute | solution.py:34
  1014.4 2.5 collective-permute-done.1
  1016.9 11.0 %collective-permute-done.3 = bf16[128,1024]{1,0:T(8,128)(2,1)S(1)} collective-permute-done((bf16[128,1024]{1,0:T(8,128)(2,1)S(1)}, bf16[128,1024]{1,0:T(8,128)(2,1)S(1)}, u32[]{:S(2)}, u32[]{:S(2)}) %collective-permute-start.3) | collective-permute-done | bytes 262176 | tf_op jit(solution)/shard_map/ppermute | solution.py:34
  (166 shorter events, 46.2 us)
Async XLA Ops:
  6.5 107.4 %copy-start = (bf16[1,128,128]{2,1,0:T(8,128)(2,1)S(1)}, bf16[1,128,128]{2,1,0:T(8,128)(2,1)}, u32[]{:S(2)}) copy-start(bf16[1,128,128]{2,1,0:T(8,128)(2,1)} %param.18) | copy-start | bytes 98308
  6.5 107.4 %copy-start.3 = (bf16[1,128,128]{2,1,0:T(8,128)(2,1)S(1)}, bf16[1,128,128]{2,1,0:T(8,128)(2,1)}, u32[]{:S(2)}) copy-start(bf16[1,128,128]{2,1,0:T(8,128)(2,1)} %param.17) | copy-start | bytes 98308
  6.5 375.4 %all-gather.10.cloned.1.call-start = ((), (), s32[]{:S(2)}) async-start(), calls=%async_computation.1 | async-start | bytes 34603008 | tf_op jit(solution)/shard_map/all_gather | solution.py:16
  12.3 226.8 %copy-start.2 = (bf16[1,128,2048]{2,1,0:T(8,128)(2,1)S(1)}, bf16[1,128,2048]{2,1,0:T(8,128)(2,1)}, u32[]{:S(2)}) copy-start(bf16[1,128,2048]{2,1,0:T(8,128)(2,1)} %param.16) | copy-start | bytes 1572868
  12.4 227.9 %copy-start.5 = (s32[16]{0:T(128)S(1)}, s32[16]{0:T(128)}, u32[]{:S(2)}) copy-start(s32[16]{0:T(128)} %param.23) | copy-start | bytes 196
  12.4 740.7 %all-gather.12.cloned.1.call-start = ((), (), s32[]{:S(2)}) async-start(), calls=%async_computation.2 | async-start | bytes 34603008 | tf_op jit(solution)/shard_map/all_gather | solution.py:16
  14.8 956.9 %all-gather.8.cloned.1.call-start = ((), (), s32[]{:S(2)}) async-start(), calls=%async_computation | async-start | bytes 4325376 | tf_op jit(solution)/shard_map/all_gather | solution.py:146
  778.2 46.8 %copy-start.1 = (f32[1,128,2048]{1,2,0:T(8,128)S(1)}, f32[1,128,2048]{1,2,0:T(8,128)}, u32[]{:S(2)}) copy-start(f32[1,128,2048]{1,2,0:T(8,128)} %copy.55) | copy-start | bytes 3145732
  825.0 1.0 copy-start.4
  975.5 18.5 %collective-permute-start = (bf16[128,1024]{1,0:T(8,128)(2,1)S(1)}, bf16[128,1024]{1,0:T(8,128)(2,1)S(1)}, u32[]{:S(2)}, u32[]{:S(2)}) collective-permute-start(bf16[128,1024]{1,0:T(8,128)(2,1)S(1)} %convolution_convert_fusion), channel_id=1, source_target_pairs={{0,32},{32,64},{64,96},{96,128},{128,160},{160,192},{192,224},{224... | collective-permute-start | bytes 786440 | tf_op jit(solution)/shard_map/ppermute | solution.py:34
  977.4 35.7 %collective-permute-start.2 = (bf16[128,1024]{1,0:T(8,128)(2,1)S(1)}, bf16[128,1024]{1,0:T(8,128)(2,1)S(1)}, u32[]{:S(2)}, u32[]{:S(2)}) collective-permute-start(bf16[128,1024]{1,0:T(8,128)(2,1)S(1)} %convolution_convert_fusion), channel_id=1, source_target_pairs={{32,0},{64,32},{96,64},{128,96},{160,128},{192,160},{224,192},{256... | collective-permute-start | bytes 786440 | tf_op jit(solution)/shard_map/ppermute | solution.py:34
  994.0 22.9 %collective-permute-start.1 = (bf16[128,1024]{1,0:T(8,128)(2,1)S(1)}, bf16[128,1024]{1,0:T(8,128)(2,1)S(1)}, u32[]{:S(2)}, u32[]{:S(2)}) collective-permute-start(bf16[128,1024]{1,0:T(8,128)(2,1)S(1)} %collective-permute-done), channel_id=1, source_target_pairs={{28,0},{29,1},{30,2},{31,3},{60,32},{61,33},{62,34},{63,35},{92,64... | collective-permute-start | bytes 786440 | tf_op jit(solution)/shard_map/ppermute | solution.py:34
  1013.1 14.9 %collective-permute-start.3 = (bf16[128,1024]{1,0:T(8,128)(2,1)S(1)}, bf16[128,1024]{1,0:T(8,128)(2,1)S(1)}, u32[]{:S(2)}, u32[]{:S(2)}) collective-permute-start(bf16[128,1024]{1,0:T(8,128)(2,1)S(1)} %collective-permute-done.2), channel_id=1, source_target_pairs={{0,28},{1,29},{2,30},{3,31},{32,60},{33,61},{34,62},{35,63},{64,92... | collective-permute-start | bytes 786440 | tf_op jit(solution)/shard_map/ppermute | solution.py:34
Sparse Core Ops, SparseCore 0:
  12.5 369.4 all-gather.9
  384.0 369.0 all-gather.11
  755.2 216.5 all-gather.7
where the time goes:
time: 1040 us
  waiting for transfers between devices  626 us (60%)
  blocking collectives  215 us (21%)
  other arithmetic  96.9 us (9%)
  starting transfers between devices  36.8 us (4%)
  local copies, waits for them, and re-layouts  27.7 us (3%)
  matrix products  18.1 us (2%)
  between operations  13.4 us (1%)
    all_gather x2, waiting for transfers between devices, prefix(): pieces = jax.tree.map(lambda part: lax.all_gather(part, axis), value)  464 us
    all_gather x2, blocking collectives, prefix(): pieces = jax.tree.map(lambda part: lax.all_gather(part, axis), value)  215 us
    all_gather x1, waiting for transfers between devices, per_device(): lax.all_gather(output_weight, 'tm', axis=1, tiled=True)  145 us
    select_n x62, other arithmetic, lap(): jnp.where(position < mine, new, old)  91 us
    ppermute x4, starting transfers between devices, shifted(): return lax.ppermute(array, axis, pairs)  36.7 us
    rev x2, local copies, waits for them, and re-layouts, prefix(): pieces = jax.tree.map(lambda part: part[::-1], pieces)  23.3 us
  transfers between devices with their start and end apart: 7, of which 6 were waited for; matrix products, arithmetic and copies ran while one was open for 13% of the time, Pallas kernels for 0%

commit v1 on v0

--- a/solution.py
+++ b/solution.py
@@ -1,3 +1,4 @@
+import functools
 import jax
 import jax.numpy as jnp
 from jax import lax
@@ -9,6 +10,21 @@
 SEAM_DEVS = 4
 STATE_LOSS = 0.4
 EPSILON = 1e-05
+
+
+def pass_loads_on_mesh(arr, dev_axis):
+    return jnp.concatenate(
+        lax.all_to_all(
+            jnp.stack([arr] * lax.axis_size(dev_axis)),
+            split_axis=0,
+            axis_name=dev_axis,
+            concat_axis=0,
+        ),
+        1,
+    )
+
+
+treat_unit = functools.partial(pass_loads_on_mesh, dev_axis="tm")
 
 
 def prefix(value, axis, join, neutral, backward):
@@ -142,9 +158,7 @@
         (gated_rows * inverse_rms).reshape(frame_count, H * P_SIZE) * gated_norm_gain[None, :]
     ).astype(jnp.bfloat16)
     projected_rows = jnp.dot(
-        normed,
-        lax.all_gather(output_weight, "tm", axis=1, tiled=True),
-        preferred_element_type=jnp.float32,
+        normed, treat_unit(output_weight), preferred_element_type=jnp.float32
     ).astype(jnp.bfloat16)
     across_previous = shifted(projected_rows, "win", 1)
     from_previous = shifted(across_previous, "tm", -reach)

time: 1040 us -> 1070 us (1.029)
  blocking collectives: 215 us -> 381 us
  waiting for transfers between devices: 626 us -> 481 us
    all_gather x2, blocking collectives: 215 us -> 381 us  [prefix(): pieces = jax.tree.map(lambda part: lax.all_gather(part, axis), value)]
    all_gather x1 -> x0, waiting for transfers between devices: 145 us -> none  [per_device(): lax.all_gather(output_weight, 'tm', axis=1, tiled=True)]
    all_to_all x0 -> x1, starting transfers between devices: none -> 12.8 us  [pass_loads_on_mesh(): lax.all_to_all(jnp.stack([arr] * lax.axis_size(dev_axis)), split_axis=0,...]
  transfers between devices with their start and end apart: 7 -> 7, of which waited for: 6 -> 5; matrix products, arithmetic and copies ran while one was open for 13% -> 13% of each run, Pallas kernels for 0% -> 0%
where the time goes in v1:
time: 1070 us; the launch traced here: 1060 us
  waiting for transfers between devices  481 us (45%)
  blocking collectives  381 us (36%)
  other arithmetic  96.6 us (9%)
  starting transfers between devices  39.6 us (4%)
  local copies, waits for them, and re-layouts  30.3 us (3%)
  matrix products  19.1 us (2%)
  between operations  13.6 us (1%)
    all_gather x2, waiting for transfers between devices, prefix(): pieces = jax.tree.map(lambda part: lax.all_gather(part, axis), value)  465 us
    all_gather x2, blocking collectives, prefix(): pieces = jax.tree.map(lambda part: lax.all_gather(part, axis), value)  381 us
    select_n x62, other arithmetic, lap(): jnp.where(position < mine, new, old)  90.8 us
    ppermute x4, starting transfers between devices, shifted(): return lax.ppermute(array, axis, pairs)  26.7 us
    rev x2, local copies, waits for them, and re-layouts, prefix(): pieces = jax.tree.map(lambda part: part[::-1], pieces)  23.3 us
  transfers between devices with their start and end apart: 7, of which 5 were waited for; matrix products, arithmetic and copies ran while one was open for 13% of the time, Pallas kernels for 0%

profile of v1, /device:TPU:480, one launch (start us, length us, event | category | flops | bytes accessed | tf_op | source)
XLA Modules:
  0.0 1063.5 jit_solution(11479082685687124059)
XLA Ops:
  10.5 1.8 convolution_bitcast_fusion.4
  13.0 1.8 convolution_bitcast_fusion.3
  14.8 2.5 stack.7
  17.4 12.8 %all-to-all-start = ((bf16[32,2048,32]{1,2,0:T(8,128)(2,1)}), bf16[32,2048,32]{1,2,0:T(8,128)(2,1)}, u32[]{:S(2)}, u32[]{:S(2)}) async-start(bf16[32,2048,32]{1,2,0:T(8,128)(2,1)} %stack.7), calls=%async_computation | async-start | bytes 8388608 | tf_op jit(solution)/shard_map/all_to_all | solution.py:17
  30.3 274.9 %all-gather.3 = f32[32,1,32]{2,1,0:T(1,128)S(1)} all-gather(f32[1,1,32]{2,1,0:T(1,128)S(1)} %get-tuple-element.324), channel_id=1, replica_groups=mesh['win'=16,'tm'=32] {'tm'}, dimensions={0}, use_global_device_ids=true | all-gather | bytes 4224 | tf_op jit(solution)/shard_map/all_gather | solution.py:32
  307.2 106.4 %all-gather.2 = f32[32,1,32]{2,1,0:T(1,128)S(1)} all-gather(f32[1,1,32]{2,1,0:T(1,128)S(1)} %get-tuple-element.328), channel_id=1, replica_groups=mesh['win'=16,'tm'=32] {'tm'}, dimensions={0}, use_global_device_ids=true | all-gather | bytes 4224 | tf_op jit(solution)/shard_map/all_gather | solution.py:32
  415.3 8.2 while.39
  423.5 84.9 %all-gather.7.cloned.1.call-done = f32[1024,64,128]{2,1,0:T(8,128)} async-done(((f32[32,64,128]{2,1,0:T(8,128)}), f32[1024,64,128]{2,1,0:T(8,128)}) %all-gather.7.cloned.1.call-update) | async-done | bytes 33554448 | tf_op jit(solution)/shard_map/all_gather | solution.py:32
  508.4 46.5 %while.40 = (s32[]{:T(128)}, f32[32,64,128]{2,1,0:T(8,128)S(1)}, s32[]{:T(128)}, f32[32,32]{1,0:T(8,128)S(1)}, f32[32,32,64,128]{3,2,1,0:T(8,128)}, /*index=5*/s32[]{:T(128)}, s32[]{:T(128)}) while((s32[]{:T(128)}, f32[32,64,128]{2,1,0:T(8,128)S(1)}, s32[]{:T(128)}, f32[32,32]{1,0:T(8,128)S(1)}, f32[32,32,64,128]{3,2,1,0:T(8,128)}, ...), condition=%wide.region_6.7_spmd.clone, body=%wide.region_5.6_spmd.clone.sunk | while | flops 1048580 | bytes 3146217 | solution.py:44
  509.9 1.5 fusion.52
  511.4 1.5 fusion.52
  512.9 1.5 fusion.52
  514.4 1.5 fusion.52
  515.9 1.5 fusion.52
  517.4 1.5 fusion.52
  518.9 1.5 fusion.52
  520.4 1.5 fusion.52
  521.9 1.5 fusion.52
  523.4 1.5 fusion.52
  524.9 1.5 fusion.52
  526.4 1.5 fusion.52
  527.9 1.5 fusion.52
  529.4 1.5 fusion.52
  532.5 1.5 fusion.52
  534.0 1.5 fusion.52
  535.5 1.5 fusion.52
  537.0 1.5 fusion.52
  538.5 1.5 fusion.52
  540.0 1.5 fusion.52
  541.5 1.5 fusion.52
  543.0 1.5 fusion.52
  544.5 1.5 fusion.52
  546.0 1.5 fusion.52
  547.5 1.5 fusion.52
  549.0 1.5 fusion.52
  550.5 1.5 fusion.52
  552.0 1.5 fusion.52
  553.5 1.5 fusion.52
  555.0 380.1 %all-gather.9.cloned.1.call-done = f32[1024,64,128]{2,1,0:T(8,128)} async-done(((f32[32,64,128]{2,1,0:T(8,128)}), f32[1024,64,128]{2,1,0:T(8,128)}) %all-gather.9.cloned.1.call-update) | async-done | bytes 33554448 | tf_op jit(solution)/shard_map/all_gather | solution.py:32
  935.0 23.3 %rev.16 = f32[32,32,64,128]{3,2,1,0:T(8,128)} reverse(f32[32,32,64,128]{3,2,1,0:T(8,128)} %bitcast.116), dimensions={0} | reverse | bytes 67108864 | tf_op jit(solution)/shard_map/rev | solution.py:34
  958.3 2.8 fusion.17
  961.2 46.7 %while.41 = (s32[]{:T(128)}, f32[32,64,128]{2,1,0:T(8,128)S(1)}, s32[]{:T(128)}, f32[32,32]{1,0:T(8,128)S(1)}, f32[32,32,64,128]{3,2,1,0:T(8,128)}, /*index=5*/s32[]{:T(128)}, s32[]{:T(128)}) while((s32[]{:T(128)}, f32[32,64,128]{2,1,0:T(8,128)S(1)}, s32[]{:T(128)}, f32[32,32]{1,0:T(8,128)S(1)}, f32[32,32,64,128]{3,2,1,0:T(8,128)}, ...), condition=%wide.region_8.9_spmd.clone, body=%wide.region_7.8_spmd.clone.sunk | while | flops 1048580 | bytes 3146217 | solution.py:44
  961.2 1.6 fusion.53
  962.8 1.5 fusion.53
  964.3 1.5 fusion.53
  965.8 1.5 fusion.53
  967.3 1.5 fusion.53
  968.8 1.5 fusion.53
  970.4 1.5 fusion.53
  971.9 1.5 fusion.53
  974.9 1.5 fusion.53
  976.4 1.5 fusion.53
  977.9 1.5 fusion.53
  979.4 1.5 fusion.53
  980.9 1.5 fusion.53
  982.4 1.5 fusion.53
  983.9 1.5 fusion.53
  1009.1 3.7 convolution_convert_fusion
  1012.8 1.9 collective-permute-start
  1014.8 14.5 %collective-permute-start.2 = (bf16[128,1024]{1,0:T(8,128)(2,1)S(1)}, bf16[128,1024]{1,0:T(8,128)(2,1)S(1)}, u32[]{:S(2)}, u32[]{:S(2)}) collective-permute-start(bf16[128,1024]{1,0:T(8,128)(2,1)S(1)} %convolution_convert_fusion), channel_id=1, source_target_pairs={{32,0},{64,32},{96,64},{128,96},{160,128},{192,160},{224,192},{256... | collective-permute-start | bytes 786440 | tf_op jit(solution)/shard_map/ppermute | solution.py:50
  1029.3 2.3 collective-permute-done
  1031.7 9.1 collective-permute-start.1
  1042.1 2.5 collective-permute-done.1
  1044.6 11.0 %collective-permute-done.3 = bf16[128,1024]{1,0:T(8,128)(2,1)S(1)} collective-permute-done((bf16[128,1024]{1,0:T(8,128)(2,1)S(1)}, bf16[128,1024]{1,0:T(8,128)(2,1)S(1)}, u32[]{:S(2)}, u32[]{:S(2)}) %collective-permute-start.3) | collective-permute-done | bytes 262176 | tf_op jit(solution)/shard_map/ppermute | solution.py:50
  (170 shorter events, 47.0 us)
Async XLA Ops:
  6.5 408.6 %copy-start = (bf16[1,128,128]{2,1,0:T(8,128)(2,1)S(1)}, bf16[1,128,128]{2,1,0:T(8,128)(2,1)}, u32[]{:S(2)}) copy-start(bf16[1,128,128]{2,1,0:T(8,128)(2,1)} %param.18) | copy-start | bytes 98308
  6.5 8.3 copy-start.4
  6.5 501.9 %all-gather.7.cloned.1.call-start = ((), (), s32[]{:S(2)}) async-start(), calls=%async_computation.1 | async-start | bytes 34603008 | tf_op jit(solution)/shard_map/all_gather | solution.py:32
  12.4 922.7 %all-gather.9.cloned.1.call-start = ((), (), s32[]{:S(2)}) async-start(), calls=%async_computation.2 | async-start | bytes 34603008 | tf_op jit(solution)/shard_map/all_gather | solution.py:32
  17.3 287.9 %copy-start.3 = (bf16[1,128,2048]{2,1,0:T(8,128)(2,1)S(1)}, bf16[1,128,2048]{2,1,0:T(8,128)(2,1)}, u32[]{:S(2)}) copy-start(bf16[1,128,2048]{2,1,0:T(8,128)(2,1)} %param.16) | copy-start | bytes 1572868
  17.3 289.1 %copy-start.6 = (f32[2048]{0:T(1024)S(1)}, f32[2048]{0:T(1024)}, u32[]{:S(2)}) copy-start(f32[2048]{0:T(1024)} %param.21) | copy-start | bytes 24580
  17.3 289.2 %copy-start.7 = (s32[16]{0:T(128)S(1)}, s32[16]{0:T(128)}, u32[]{:S(2)}) copy-start(s32[16]{0:T(128)} %param.23) | copy-start | bytes 196
  17.3 397.8 %copy-start.5 = (bf16[1,128,128]{2,1,0:T(8,128)(2,1)S(1)}, bf16[1,128,128]{2,1,0:T(8,128)(2,1)}, u32[]{:S(2)}) copy-start(bf16[1,128,128]{2,1,0:T(8,128)(2,1)} %param.17) | copy-start | bytes 98308
  17.4 991.8 %all-to-all-start = ((bf16[32,2048,32]{1,2,0:T(8,128)(2,1)}), bf16[32,2048,32]{1,2,0:T(8,128)(2,1)}, u32[]{:S(2)}, u32[]{:S(2)}) async-start(bf16[32,2048,32]{1,2,0:T(8,128)(2,1)} %stack.7), calls=%async_computation | async-start | bytes 8388608 | tf_op jit(solution)/shard_map/all_to_all | solution.py:17
  961.2 46.7 %copy-start.1 = (f32[128,32,64]{0,2,1:T(8,128)S(1)}, f32[128,32,64]{0,2,1:T(8,128)}, u32[]{:S(2)}) copy-start(f32[128,32,64]{0,2,1:T(8,128)} %fusion.17) | copy-start | bytes 3145732
  961.2 46.7 %copy-start.2 = (f32[1,128,2048]{1,2,0:T(8,128)S(1)}, f32[1,128,2048]{1,2,0:T(8,128)}, u32[]{:S(2)}) copy-start(f32[1,128,2048]{1,2,0:T(8,128)} %copy.56) | copy-start | bytes 3145732
  1012.8 18.8 %collective-permute-start = (bf16[128,1024]{1,0:T(8,128)(2,1)S(1)}, bf16[128,1024]{1,0:T(8,128)(2,1)S(1)}, u32[]{:S(2)}, u32[]{:S(2)}) collective-permute-start(bf16[128,1024]{1,0:T(8,128)(2,1)S(1)} %convolution_convert_fusion), channel_id=1, source_target_pairs={{0,32},{32,64},{64,96},{96,128},{128,160},{160,192},{192,224},{224... | collective-permute-start | bytes 786440 | tf_op jit(solution)/shard_map/ppermute | solution.py:50
  1014.8 26.0 %collective-permute-start.2 = (bf16[128,1024]{1,0:T(8,128)(2,1)S(1)}, bf16[128,1024]{1,0:T(8,128)(2,1)S(1)}, u32[]{:S(2)}, u32[]{:S(2)}) collective-permute-start(bf16[128,1024]{1,0:T(8,128)(2,1)S(1)} %convolution_convert_fusion), channel_id=1, source_target_pairs={{32,0},{64,32},{96,64},{128,96},{160,128},{192,160},{224,192},{256... | collective-permute-start | bytes 786440 | tf_op jit(solution)/shard_map/ppermute | solution.py:50
  1031.7 12.9 %collective-permute-start.1 = (bf16[128,1024]{1,0:T(8,128)(2,1)S(1)}, bf16[128,1024]{1,0:T(8,128)(2,1)S(1)}, u32[]{:S(2)}, u32[]{:S(2)}) collective-permute-start(bf16[128,1024]{1,0:T(8,128)(2,1)S(1)} %collective-permute-done), channel_id=1, source_target_pairs={{28,0},{29,1},{30,2},{31,3},{60,32},{61,33},{62,34},{63,35},{92,64... | collective-permute-start | bytes 786440 | tf_op jit(solution)/shard_map/ppermute | solution.py:50
  1040.8 14.9 %collective-permute-start.3 = (bf16[128,1024]{1,0:T(8,128)(2,1)S(1)}, bf16[128,1024]{1,0:T(8,128)(2,1)S(1)}, u32[]{:S(2)}, u32[]{:S(2)}) collective-permute-start(bf16[128,1024]{1,0:T(8,128)(2,1)S(1)} %collective-permute-done.2), channel_id=1, source_target_pairs={{0,28},{1,29},{2,30},{3,31},{32,60},{33,61},{34,62},{35,63},{64,92... | collective-permute-start | bytes 786440 | tf_op jit(solution)/shard_map/ppermute | solution.py:50
Sparse Core Ops, SparseCore 0:
  12.5 495.8 all-gather.6
  510.5 424.5 all-gather.8
